TPU v7x, 256 devices: a whole 4x4x8 slice. The times are simulated.
256 devices in a mesh: req: 128 (over x, y, z), tp: 2 (over core).
Axes of the slice: x: 4, y: 4, z: 8, core: 2. Of those that a mesh axis runs over, the one named last changes fastest.
Arguments:
- tokens: bfloat16 [65536, 1024], P('req'), may hold values from -6 to 6
- group_len: int32 [128], P('req'), may hold values from 1 to 512, 49152 in all
- cache_len: int32 [128], replicated, may hold values from 1 to 1024, 65536 in all
- cache_keys: bfloat16 [128, 1024, 1024], P('req', None, 'tp'), may hold values from -192 to 192
- cache_values: bfloat16 [128, 1024, 1024], P('req', None, 'tp'), may hold values from -6 to 6
- w_query: bfloat16 [1024, 1024], P(None, 'tp'), may hold values from -0.1875 to 0.1875
- w_key: bfloat16 [1024, 1024], P(None, 'tp'), may hold values from -0.1875 to 0.1875
- w_value: bfloat16 [1024, 1024], P(None, 'tp'), may hold values from -0.1875 to 0.1875
- w_out: bfloat16 [1024, 1024], P('tp'), may hold values from -0.1875 to 0.1875
- w_up: bfloat16 [1024, 2048], P(None, 'tp'), may hold values from -0.1875 to 0.1875
- w_down: bfloat16 [2048, 1024], P('tp'), may hold values from -0.125 to 0.125
- ln_gains: float32 [2, 1024], replicated, may hold values from 0.5 to 1.5
- ln_biases: float32 [2, 1024], replicated, may hold values from -3 to 3
- embed: bfloat16 [49152, 1024], P(('req', 'tp')), may hold values from -0.5 to 0.5
Outputs:
- layer_out: bfloat16 [65536, 1024], P('req')
- top_logit: float32 [128], P('req')
- shard_top: float32 [128, 256], P(None, ('req', 'tp'))
Inputs may be any that keep to these rules, and one draw needn't show every extreme that they name: `cache_len`: one request has exactly 1024 cached positions. `group_len`: one request has a full block of 512 valid tokens.
All inputs are finite; a program needn't handle non-finite values.
Results may differ from a plain program's by a relative error of at most 0.015.
Values may be sent and summed in bfloat16 or wider, within the bound.
No kernel may reach another device: no remote copies, remote signals or barrier semaphores. Data moves between devices by JAX's collectives and lax.ppermute only.
A program may use at most 128 MiB of HBM per device.

v0:
```python
import jax
import jax.numpy as jnp
from jax import lax
from jax.sharding import PartitionSpec as P

HD = 64
BLK = 256
start_peak = -1e30


def normalize(rows, gain, bias):
    center = rows - jnp.mean(rows, axis=-1, keepdims=True)
    spread = jnp.mean(center * center, axis=-1, keepdims=True)
    return center * lax.rsqrt(spread + 1e-05) * gain + bias


def attend(soft_state, queries, keys_blk, values_blk, allowed):
    row_peak, row_total, accum = soft_state
    scale = 1.0 / jnp.sqrt(jnp.float32(queries.shape[2]))
    scores = (
        jnp.einsum("qhd,khd->qhk", queries, keys_blk, preferred_element_type=jnp.float32) * scale
    )
    scores = jnp.where(allowed[:, None, :], scores, -jnp.inf)
    new_peak = jnp.maximum(row_peak, jnp.max(scores, axis=-1))
    factor = jnp.exp(row_peak - new_peak)
    raised = jnp.exp(scores - new_peak[..., None])
    new_total = row_total * factor + jnp.sum(raised, axis=-1)
    new_accum = accum * factor[..., None] + jnp.einsum(
        "qhk,khd->qhd", raised.astype(jnp.bfloat16), values_blk, preferred_element_type=jnp.float32
    )
    return (new_peak, new_total, new_accum)


def cache_pass(soft_state, queries, keys_all, values_all, offset, blocks, length):

    def one_block(block_idx, carry):
        keys_blk = lax.dynamic_slice_in_dim(keys_all, block_idx * BLK, BLK, 0)
        values_blk = lax.dynamic_slice_in_dim(values_all, block_idx * BLK, BLK, 0)
        places = offset + block_idx * BLK + jnp.arange(BLK, dtype=jnp.int32)
        return attend(carry, queries, keys_blk, values_blk, (places < length)[None, :])

    return lax.fori_loop(jnp.int32(0), blocks, one_block, soft_state)


def shards(
    tokens,
    group_len,
    cache_len,
    cache_keys,
    cache_values,
    w_query,
    w_key,
    w_value,
    w_out,
    w_up,
    w_down,
    ln_gains,
    ln_biases,
    embed,
):
    block_rows = tokens.shape[0]
    local_width = w_query.shape[1]
    heads_local = local_width // HD
    cache_rows = cache_keys.shape[1]
    my_index = lax.axis_index("req")
    my_cache = lax.dynamic_index_in_dim(cache_len, my_index, 0, keepdims=False)
    my_valid = group_len[0]
    queries = jnp.dot(tokens, w_query, preferred_element_type=jnp.float32).astype(jnp.bfloat16)
    keys_new = jnp.dot(tokens, w_key, preferred_element_type=jnp.float32).astype(jnp.bfloat16)
    values_new = jnp.dot(tokens, w_value, preferred_element_type=jnp.float32).astype(jnp.bfloat16)
    head_queries = queries.reshape(block_rows, heads_local, HD)
    empty_state = (
        jnp.full((block_rows, heads_local), start_peak, jnp.float32),
        jnp.zeros((block_rows, heads_local), jnp.float32),
        jnp.zeros((block_rows, heads_local, HD), jnp.float32),
    )
    row_ids = jnp.arange(block_rows, dtype=jnp.int32)
    block_allowed = (row_ids[None, :] <= row_ids[:, None]) & (row_ids < my_valid)[None, :]
    soft_state = attend(
        empty_state,
        head_queries,
        keys_new.reshape(block_rows, heads_local, HD),
        values_new.reshape(block_rows, heads_local, HD),
        block_allowed,
    )
    own_keys = cache_keys[0].reshape(cache_rows, heads_local, HD)
    own_values = cache_values[0].reshape(cache_rows, heads_local, HD)
    own_blocks = (my_cache + BLK - 1) // BLK
    soft_state = cache_pass(soft_state, head_queries, own_keys, own_values, 0, own_blocks, my_cache)
    attn_mixed = (
        (soft_state[2] / soft_state[1][..., None])
        .astype(jnp.bfloat16)
        .reshape(block_rows, local_width)
    )
    attn_sum = lax.psum(
        jnp.dot(attn_mixed, w_out, preferred_element_type=jnp.float32).astype(jnp.bfloat16), "tp"
    ).astype(jnp.float32)
    middle = normalize(tokens.astype(jnp.float32) + attn_sum, ln_gains[0], ln_biases[0]).astype(
        jnp.bfloat16
    )
    active = jax.nn.gelu(
        jnp.dot(middle, w_up, preferred_element_type=jnp.float32), approximate=False
    ).astype(jnp.bfloat16)
    ffn_sum = lax.psum(
        jnp.dot(active, w_down, preferred_element_type=jnp.float32).astype(jnp.bfloat16), "tp"
    ).astype(jnp.float32)
    layer_out = normalize(middle.astype(jnp.float32) + ffn_sum, ln_gains[1], ln_biases[1]).astype(
        jnp.bfloat16
    )
    last_row = lax.dynamic_slice_in_dim(layer_out, my_valid - 1, 1, 0)
    logits = jnp.einsum(
        "rd,vd->rv",
        lax.all_gather(last_row, "req", axis=0, tiled=True),
        embed,
        preferred_element_type=jnp.float32,
    )
    slice_best = jnp.max(logits, axis=1)
    best_logit = lax.pmax(slice_best, ("req", "tp"))
    return (layer_out, lax.dynamic_slice_in_dim(best_logit, my_index, 1, 0), slice_best[:, None])


def solution(mesh):
    placed = (
        P("req", None),
        P("req"),
        P(),
        P("req", None, "tp"),
        P("req", None, "tp"),
        P(None, "tp"),
        P(None, "tp"),
        P(None, "tp"),
        P("tp", None),
        P(None, "tp"),
        P("tp", None),
        P(),
        P(),
        P(("req", "tp"), None),
    )
    return jax.shard_map(
        shards,
        mesh=mesh,
        in_specs=placed,
        out_specs=(P("req", None), P("req"), P(None, ("req", "tp"))),
        check_vma=False,
    )
```

profile of v0, /device:TPU:1, one launch (start us, length us, event | category | flops | bytes accessed | tf_op | source)
XLA Modules:
  0.0 564.5 jit_solution(3807487911290846801)
XLA Ops:
  7.2 1.5 dynamic_slice.16
  10.3 2.3 convolution_convert_fusion.4
  13.4 1.5 fusion.24
  14.9 1.7 fusion.23
  18.1 1.6 convolution_convert_fusion.2
  19.7 2.4 copy.27
  23.4 5.7 %fusion.45 = f32[512,8,64]{0,2,1:T(8,128)S(1)} fusion(bf16[512,8,64]{0,2,1:T(8,128)(2,1)} %bitcast.92, f32[8,512,512]{2,1,0:T(8,128)} %copy-done.1, f32[512,8]{0,1:T(8,128)S(1)} %broadcast_maximum_fusion, pred[512,512]{0,1:T(8,128)(4,1)S(1)} %fusion.79, f32[512,8]{0,1:T(8,128)S(1)} %get-tuple-element.76), kind=kOutput, calls=%fused_computation.62 | convolution fusion | flops 277086208 | bytes 10256384 | tf_op jit(solution)/shard_map/qhk,khd->qhd/dot_general | solution.py:28
  29.2 23.9 %while.14 = (s32[]{:T(128)}, f32[512,8]{0,1:T(8,128)S(1)}, f32[512,8]{0,1:T(8,128)S(1)}, f32[512,8,64]{0,2,1:T(8,128)S(1)}, s32[]{:T(128)}, /*index=5*/s32[]{:T(...) while((s32[]{:T(128)}, f32[512,8]{0,1:T(8,128)S(1)}, ...), condition=%wide.region_5.6_spmd, body=%wide.region_2.5_spmd.sunk | while | flops 280502784 | bytes 15992003 | solution.py:42
  29.9 2.1 bitcast_reduce_fusion.2
  33.0 2.1 fusion.144
  35.8 2.1 bitcast_reduce_fusion.2
  38.9 2.1 fusion.144
  41.8 2.1 bitcast_reduce_fusion.2
  44.8 2.1 fusion.144
  47.7 2.1 bitcast_reduce_fusion.2
  50.8 2.1 fusion.144
  53.3 3.0 convolution_convert_fusion.1
  56.4 34.8 %all-reduce.3.cloned.1.call-done = bf16[512,1024]{1,0:T(8,128)(2,1)} async-done(((bf16[512,1024]{1,0:T(8,128)(2,1)}), bf16[512,1024]{1,0:T(8,128)(2,1)}) %all-reduce.3.cloned.1.call-update) | async-done | bytes 1048592 | tf_op jit(solution)/shard_map/psum | solution.py:95
  91.2 1.7 fusion.39
  94.0 8.8 %convolution_convert_fusion = bf16[512,1024]{1,0:T(8,128)(2,1)} fusion(bf16[1024,1024]{1,0:T(8,128)(2,1)S(1)} %copy-done, bf16[512,1024]{1,0:T(8,128)(2,1)S(1)} %add_convert_fusion.1, bf16[1024,1024]{1,0:T(8,128)(2,1)} %param.25), kind=kOutput, calls=%fused_computation.59 | convolution fusion | flops 2182086656 | bytes 6291456 | tf_op jit(solution)/shard_map/dot_general | solution.py:105
  102.9 31.7 %all-reduce.5.cloned.1.call-done = bf16[512,1024]{1,0:T(8,128)(2,1)} async-done(((bf16[512,1024]{1,0:T(8,128)(2,1)}), bf16[512,1024]{1,0:T(8,128)(2,1)}) %all-reduce.5.cloned.1.call-update) | async-done | bytes 1048592 | tf_op jit(solution)/shard_map/psum | solution.py:104
  134.6 1.7 fusion.41
  138.3 292.9 %all-gather = bf16[128,1,1024]{2,1,0:T(2,128)(2,1)S(1)} all-gather(bf16[1,1,1024]{2,1,0:T(2,128)(2,1)S(1)} %dynamic-slice_bitcast_fusion), channel_id=1, replica_groups=mesh['req'=128,'tp'=2] {'req'}, dimensions={0}, use_global_device_ids=true | all-gather | bytes 264192 | tf_op jit(solution)/shard_map/all_gather | solution.py:113
  431.5 125.6 %pmax.7 = f32[128]{0:T(128)S(1)} all-reduce(f32[128]{0:T(128)S(1)} %convolution_reduce_fusion), channel_id=1, replica_groups=mesh['req'=128,'tp'=2] {'req','tp'}, use_global_device_ids=true, to_apply=%region_13.14 | all-reduce | flops 128 | bytes 1024 | tf_op jit(solution)/shard_map/pmax | solution.py:118
  (76 shorter events, 14.5 us)
Async XLA Ops:
  7.2 86.9 %copy-start = (bf16[1024,1024]{1,0:T(8,128)(2,1)S(1)}, bf16[1024,1024]{1,0:T(8,128)(2,1)}, u32[]{:S(2)}) copy-start(bf16[1024,1024]{1,0:T(8,128)(2,1)} %param.26) | copy-start | bytes 6291460
  7.2 5.4 copy-start.3
  7.2 84.0 %all-reduce.3.cloned.1.call-start = ((), (), s32[]{:S(2)}) async-start(), calls=%async_computation | async-start | bytes 2097152 | tf_op jit(solution)/shard_map/psum | solution.py:95
  9.4 3.2 copy-start.12
  13.4 1.5 copy-start.2
  14.9 3.2 copy-start.1
  14.9 3.2 copy-start.13
  19.7 2.4 copy-start.9
  53.3 3.1 copy-start.10
  53.3 3.1 copy-start.11
  53.3 37.9 %copy-start.4 = (bf16[512,1024]{1,0:T(8,128)(2,1)S(1)}, bf16[512,1024]{1,0:T(8,128)(2,1)}, u32[]{:S(2)}) copy-start(bf16[512,1024]{1,0:T(8,128)(2,1)} %param.16) | copy-start | bytes 3145732
  56.3 78.2 %all-reduce.5.cloned.1.call-start = ((), (), s32[]{:S(2)}) async-start(), calls=%async_computation.1 | async-start | bytes 2097152 | tf_op jit(solution)/shard_map/psum | solution.py:104
  91.2 1.7 copy-start.7
  91.2 2.2 copy-start.5
  134.6 1.7 copy-start.6
  136.7 294.4 %copy-start.14 = (bf16[192,1024]{1,0:T(8,128)(2,1)S(1)}, bf16[192,1024]{1,0:T(8,128)(2,1)}, u32[]{:S(2)}) copy-start(bf16[192,1024]{1,0:T(8,128)(2,1)} %param.29) | copy-start | bytes 1179652
  137.3 1.0 copy-start.8
  431.5 126.2 %copy-start.15 = (f32[128]{0:T(128)}, f32[128]{0:T(128)S(1)}, u32[]{:S(2)}) copy-start(f32[128]{0:T(128)S(1)} %convolution_reduce_fusion) | copy-start | bytes 1540
Sparse Core Ops, SparseCore 0:
  56.5 34.7 all-reduce.2
  103.0 31.5 all-reduce.4
where the time goes:
time: 565 us
  blocking collectives  419 us (74%)
  waiting for transfers between devices  66.5 us (12%)
  matrix products  40.9 us (7%)
  between operations  15.8 us (3%)
  other arithmetic  14 us (2%)
  local copies, waits for them, and re-layouts  8.34 us (1%)
    all_gather x1, blocking collectives, shards(): lax.all_gather(last_row, 'req', axis=0, tiled=True)  293 us
    pmax x1, blocking collectives, shards(): best_logit = lax.pmax(slice_best, ('req', 'tp'))  126 us
    psum x1, waiting for transfers between devices, shards(): lax.psum(jnp.dot(attn_mixed, w_out, preferred_element_type=jnp.float32).a...  34.8 us
    psum x1, waiting for transfers between devices, shards(): lax.psum(jnp.dot(active, w_down, preferred_element_type=jnp.float32).asty...  31.7 us
    dot_general x5, matrix products, attend(): jnp.einsum('qhk,khd->qhd', raised.astype(jnp.bfloat16), values_blk, prefe...  14.3 us
  transfers between devices with their start and end apart: 2, of which 2 were waited for; matrix products, arithmetic and copies ran while one was open for 0% of the time, Pallas kernels for 0%

commit v1 on v0

--- a/solution.py
+++ b/solution.py
@@ -1,3 +1,4 @@
+import functools
 import jax
 import jax.numpy as jnp
 from jax import lax
@@ -6,6 +7,15 @@
 HD = 64
 BLK = 256
 start_peak = -1e30
+
+
+def raise_the_pipes(q_in, bus_axis):
+    return jnp.concatenate(
+        lax.all_to_all(jnp.stack(lax.axis_size(bus_axis) * [q_in], axis=0), bus_axis, 0, 0), axis=0
+    )
+
+
+enter_numbers_all = functools.partial(raise_the_pipes, bus_axis="req")
 
 
 def normalize(rows, gain, bias):
@@ -109,10 +119,7 @@
     )
     last_row = lax.dynamic_slice_in_dim(layer_out, my_valid - 1, 1, 0)
     logits = jnp.einsum(
-        "rd,vd->rv",
-        lax.all_gather(last_row, "req", axis=0, tiled=True),
-        embed,
-        preferred_element_type=jnp.float32,
+        "rd,vd->rv", enter_numbers_all(last_row), embed, preferred_element_type=jnp.float32
     )
     slice_best = jnp.max(logits, axis=1)
     best_logit = lax.pmax(slice_best, ("req", "tp"))

time: 565 us -> 250 us (0.44)
  blocking collectives: 419 us -> 100 us
    all_gather x1 -> x0, blocking collectives: 293 us -> none  [shards(): lax.all_gather(last_row, 'req', axis=0, tiled=True)]
    pmax x1, blocking collectives: 126 us -> 72.4 us  [shards(): best_logit = lax.pmax(slice_best, ('req', 'tp'))]
    all_to_all x0 -> x1, blocking collectives: none -> 27.8 us  [raise_the_pipes(): lax.all_to_all(jnp.stack(lax.axis_size(bus_axis) * [q_in], axis=0), bus_a...]
where the time goes in v1:
time: 250 us
  blocking collectives  100 us (40%)
  waiting for transfers between devices  66.5 us (27%)
  matrix products  40.9 us (16%)
  other arithmetic  16.1 us (6%)
  between operations  15.8 us (6%)
  local copies, waits for them, and re-layouts  9.55 us (4%)
    pmax x1, blocking collectives, shards(): best_logit = lax.pmax(slice_best, ('req', 'tp'))  72.4 us
    psum x1, waiting for transfers between devices, shards(): lax.psum(jnp.dot(attn_mixed, w_out, preferred_element_type=jnp.float32).a...  34.8 us
    psum x1, waiting for transfers between devices, shards(): lax.psum(jnp.dot(active, w_down, preferred_element_type=jnp.float32).asty...  31.7 us
    all_to_all x1, blocking collectives, raise_the_pipes(): lax.all_to_all(jnp.stack(lax.axis_size(bus_axis) * [q_in], axis=0), bus_a...  27.8 us
    dot_general x5, matrix products, attend(): jnp.einsum('qhk,khd->qhd', raised.astype(jnp.bfloat16), values_blk, prefe...  14.3 us
    dot_general x5, matrix products, attend(): jnp.einsum('qhd,khd->qhk', queries, keys_blk, preferred_element_type=jnp....  9.87 us
    dot_general x1, matrix products, shards(): jnp.dot(active, w_down, preferred_element_type=jnp.float32)  8.8 us
    unnamed x36, local copies, waits for them, and re-layouts  6.64 us
  transfers between devices with their start and end apart: 2, of which 2 were waited for; matrix products, arithmetic and copies ran while one was open for 0% of the time, Pallas kernels for 0%

profile of v1, /device:TPU:1, one launch (start us, length us, event | category | flops | bytes accessed | tf_op | source)
XLA Modules:
  0.0 249.7 jit_solution(926007348870213204)
XLA Ops:
  7.2 1.5 dynamic_slice.18
  10.3 2.3 convolution_convert_fusion.4
  14.9 1.7 fusion.23
  18.1 1.6 convolution_convert_fusion.2
  19.7 2.4 copy.27
  23.4 5.7 %fusion.45 = f32[512,8,64]{0,2,1:T(8,128)S(1)} fusion(bf16[512,8,64]{0,2,1:T(8,128)(2,1)} %bitcast.90, f32[8,512,512]{2,1,0:T(8,128)} %copy-done.1, f32[512,8]{0,1:T(8,128)S(1)} %broadcast_maximum_fusion, pred[512,512]{0,1:T(8,128)(4,1)S(1)} %fusion.79, f32[512,8]{0,1:T(8,128)S(1)} %get-tuple-element.76), kind=kOutput, calls=%fused_computation.62 | convolution fusion | flops 277086208 | bytes 10256384 | tf_op jit(solution)/shard_map/qhk,khd->qhd/dot_general | solution.py:38
  29.2 23.9 %while.14 = (s32[]{:T(128)}, f32[512,8]{0,1:T(8,128)S(1)}, f32[512,8]{0,1:T(8,128)S(1)}, f32[512,8,64]{0,2,1:T(8,128)S(1)}, s32[]{:T(128)}, /*index=5*/s32[]{:T(...) while((s32[]{:T(128)}, f32[512,8]{0,1:T(8,128)S(1)}, ...), condition=%wide.region_5.6_spmd, body=%wide.region_2.5_spmd.sunk | while | flops 280502784 | bytes 15992003 | solution.py:52
  29.9 2.1 bitcast_reduce_fusion.2
  33.0 2.1 fusion.144
  35.8 2.1 bitcast_reduce_fusion.2
  38.9 2.1 fusion.144
  41.8 2.1 bitcast_reduce_fusion.2
  44.8 2.1 fusion.144
  47.7 2.1 bitcast_reduce_fusion.2
  50.8 2.1 fusion.144
  53.3 3.0 %convolution_convert_fusion.1 = bf16[512,1024]{1,0:T(8,128)(2,1)} fusion(bf16[512,512]{0,1:T(8,128)(2,1)S(1)} %bitcast.85, bf16[512,1024]{1,0:T(8,128)(2,1)} %param.24), kind=kOutput, calls=%fused_computation.60 | convolution fusion | flops 537395200 | bytes 2621440 | tf_op jit(solution)/shard_map/dot_general | solution.py:106
  56.4 34.8 %all-reduce.3.cloned.1.call-done = bf16[512,1024]{1,0:T(8,128)(2,1)} async-done(((bf16[512,1024]{1,0:T(8,128)(2,1)}), bf16[512,1024]{1,0:T(8,128)(2,1)}) %all-reduce.3.cloned.1.call-update) | async-done | bytes 1048592 | tf_op jit(solution)/shard_map/psum | solution.py:105
  91.2 1.7 fusion.39
  94.0 8.8 %convolution_convert_fusion = bf16[512,1024]{1,0:T(8,128)(2,1)} fusion(bf16[1024,1024]{1,0:T(8,128)(2,1)S(1)} %copy-done, bf16[512,1024]{1,0:T(8,128)(2,1)S(1)} %add_convert_fusion.1, bf16[1024,1024]{1,0:T(8,128)(2,1)} %param.25), kind=kOutput, calls=%fused_computation.59 | convolution fusion | flops 2182086656 | bytes 6291456 | tf_op jit(solution)/shard_map/dot_general | solution.py:115
  102.9 31.7 %all-reduce.5.cloned.1.call-done = bf16[512,1024]{1,0:T(8,128)(2,1)} async-done(((bf16[512,1024]{1,0:T(8,128)(2,1)}), bf16[512,1024]{1,0:T(8,128)(2,1)}) %all-reduce.5.cloned.1.call-update) | async-done | bytes 1048592 | tf_op jit(solution)/shard_map/psum | solution.py:114
  134.6 1.7 fusion.41
  139.1 2.1 reduce.2
  141.4 27.8 %all_to_all.5 = bf16[128,2,512]{2,1,0:T(2,128)(2,1)S(1)} all-to-all(bf16[128,2,512]{2,1,0:T(2,128)(2,1)S(1)} %reshape.96), channel_id=1, replica_groups=mesh['req'=128,'tp'=2] {'req'}, dimensions={0} | all-to-all | bytes 524288 | tf_op jit(solution)/shard_map/all_to_all | solution.py:14
  169.8 72.4 %pmax.7 = f32[128]{0:T(128)S(1)} all-reduce(f32[128]{0:T(128)S(1)} %convolution_reduce_fusion), channel_id=1, replica_groups=mesh['req'=128,'tp'=2] {'req','tp'}, use_global_device_ids=true, to_apply=%region_13.14 | all-reduce | flops 128 | bytes 1024 | tf_op jit(solution)/shard_map/pmax | solution.py:125
  (81 shorter events, 17.2 us)
Async XLA Ops:
  7.2 86.9 %copy-start = (bf16[1024,1024]{1,0:T(8,128)(2,1)S(1)}, bf16[1024,1024]{1,0:T(8,128)(2,1)}, u32[]{:S(2)}) copy-start(bf16[1024,1024]{1,0:T(8,128)(2,1)} %param.26) | copy-start | bytes 6291460
  7.2 5.4 %copy-start.3 = (bf16[512,1024]{1,0:T(8,128)(2,1)S(1)}, bf16[512,1024]{1,0:T(8,128)(2,1)}, u32[]{:S(2)}) copy-start(bf16[512,1024]{1,0:T(8,128)(2,1)} %param.16) | copy-start | bytes 3145732
  7.2 84.0 %all-reduce.3.cloned.1.call-start = ((), (), s32[]{:S(2)}) async-start(), calls=%async_computation.1 | async-start | bytes 2097152 | tf_op jit(solution)/shard_map/psum | solution.py:105
  9.4 3.2 %copy-start.12 = (bf16[1024,512]{1,0:T(8,128)(2,1)S(1)}, bf16[1024,512]{1,0:T(8,128)(2,1)}, u32[]{:S(2)}) copy-start(bf16[1024,512]{1,0:T(8,128)(2,1)} %param.21) | copy-start | bytes 3145732
  13.4 1.5 copy-start.2
  14.9 3.2 %copy-start.1 = (f32[8,512,512]{2,1,0:T(8,128)}, f32[8,512,512]{2,1,0:T(8,128)S(1)}, u32[]{:S(2)}) copy-start(f32[8,512,512]{2,1,0:T(8,128)S(1)} %get-tuple-element.83) | copy-start | bytes 25165828
  14.9 3.2 %copy-start.13 = (bf16[1024,512]{1,0:T(8,128)(2,1)S(1)}, bf16[1024,512]{1,0:T(8,128)(2,1)}, u32[]{:S(2)}) copy-start(bf16[1024,512]{1,0:T(8,128)(2,1)} %param.23) | copy-start | bytes 3145732
  19.7 2.4 copy-start.9
  53.3 3.1 %copy-start.10 = (f32[2,1024]{1,0:T(2,128)S(1)}, f32[2,1024]{1,0:T(2,128)}, u32[]{:S(2)}) copy-start(f32[2,1024]{1,0:T(2,128)} %param.28) | copy-start | bytes 24580
  53.3 3.1 %copy-start.11 = (f32[2,1024]{1,0:T(2,128)S(1)}, f32[2,1024]{1,0:T(2,128)}, u32[]{:S(2)}) copy-start(f32[2,1024]{1,0:T(2,128)} %param.27) | copy-start | bytes 24580
  53.3 37.9 %copy-start.4 = (bf16[512,1024]{1,0:T(8,128)(2,1)S(1)}, bf16[512,1024]{1,0:T(8,128)(2,1)}, u32[]{:S(2)}) copy-start(bf16[512,1024]{1,0:T(8,128)(2,1)} %param.16) | copy-start | bytes 3145732
  56.3 78.2 %all-reduce.5.cloned.1.call-start = ((), (), s32[]{:S(2)}) async-start(), calls=%async_computation.2 | async-start | bytes 2097152 | tf_op jit(solution)/shard_map/psum | solution.py:114
  91.2 1.7 copy-start.7
  91.2 2.2 copy-start.5
  134.6 1.7 copy-start.6
  137.3 1.0 copy-start.8
  138.3 31.2 %copy-start.14 = (bf16[192,1024]{1,0:T(8,128)(2,1)S(1)}, bf16[192,1024]{1,0:T(8,128)(2,1)}, u32[]{:S(2)}) copy-start(bf16[192,1024]{1,0:T(8,128)(2,1)} %param.29) | copy-start | bytes 1179652
  169.8 73.0 %copy-start.15 = (f32[128]{0:T(128)}, f32[128]{0:T(128)S(1)}, u32[]{:S(2)}) copy-start(f32[128]{0:T(128)S(1)} %convolution_reduce_fusion) | copy-start | bytes 1540
Sparse Core Ops, SparseCore 0:
  56.5 34.7 all-reduce.2
  103.0 31.5 all-reduce.4
